TPU v7x, 512 devices: a whole 4x4x16 slice. The times are simulated.
512 devices in a mesh: req: 32 (over y, x, core), mlp: 16 (over z).
Axes of the slice: x: 4, y: 4, z: 16, core: 2. Of those that a mesh axis runs over, the one named last changes fastest.
Arguments:
- queries: bfloat16 [12288, 4096], P('req', 'mlp')
- new_keys: bfloat16 [12288, 1024], P(('req', 'mlp')), may hold values from -5 to 5
- new_values: bfloat16 [12288, 1024], P(('req', 'mlp')), may hold values from -6 to 6
- cache_keys: bfloat16 [32, 4096, 1024], P('req', 'mlp')
- cache_values: bfloat16 [32, 4096, 1024], P('req', 'mlp'), may hold values from -6 to 6
- cache_len: int32 [32], P('req'), may hold values from 256 to 4096, as said below
- residual: bfloat16 [12288, 2560], P('req')
- out_weight: bfloat16 [4096, 2560], P('mlp'), may hold values from -0.1796875 to 0.1796875
- norm_gain: bfloat16 [2560], replicated, may hold values from 0.099609375 to 1.8984375
- gate_weight: bfloat16 [2560, 9728], P('req', 'mlp'), may hold values from -0.125 to 0.125
- up_weight: bfloat16 [2560, 9728], P('req', 'mlp'), may hold values from -0.125 to 0.125
- down_weight: bfloat16 [2560, 9728], P('req', 'mlp'), may hold values from -0.0625 to 0.0625
Outputs:
- layer_out: bfloat16 [12288, 2560], P(('req', 'mlp'))
Inputs may be any that keep to these rules, and one draw needn't show every extreme that they name: cache_len[r] counts request r's valid cached positions from the first; some request has exactly 4096.
All inputs are finite; a program needn't handle non-finite values.
Results may differ from a plain program's by a relative error of at most 0.012.
Values may be sent and summed in bfloat16 or wider, within the bound.
No kernel may reach another device: no remote copies, remote signals or barrier semaphores. Data moves between devices by JAX's collectives and lax.ppermute only.
A program may use at most 64 MiB of HBM per device.

v0:
```python
import jax
import jax.numpy as jnp
from jax import lax
from jax.sharding import PartitionSpec as P

H = 32
KVH = 8
HD = 128
norm_eps = 1e-06


def shards(
    queries,
    new_keys,
    new_values,
    cache_keys,
    cache_values,
    cache_len,
    residual,
    out_weight,
    norm_gain,
    gate_weight,
    up_weight,
    down_weight,
):
    n_mlp = lax.axis_size("mlp")
    heads_dev = H // n_mlp
    group_size = H // KVH
    copies = n_mlp // KVH
    assert copies == 2 and heads_dev * copies == group_size
    query_rows = queries.shape[0]
    rows_dev = new_keys.shape[0]
    cache_dev = cache_keys.shape[1]
    cache_half = cache_dev // copies
    new_half = rows_dev // copies
    my_index = lax.axis_index("mlp")
    my_half = my_index % copies

    def to_slots(rows_block, half_rows):
        spread = rows_block.reshape(copies, half_rows, KVH, HD).transpose(1, 2, 0, 3)
        return spread.reshape(half_rows, KVH * copies, HD)

    send = jnp.concatenate(
        [
            to_slots(cache_keys[0], cache_half),
            to_slots(cache_values[0], cache_half),
            to_slots(new_keys, new_half),
            to_slots(new_values, new_half),
        ],
        axis=0,
    )
    arrived = lax.all_to_all(send, "mlp", split_axis=1, concat_axis=0, tiled=True)
    per_src = 2 * cache_half + 2 * new_half
    arrived = arrived.reshape(n_mlp, per_src, HD)
    keys_old = arrived[:, :cache_half].reshape(n_mlp * cache_half, HD)
    values_old = arrived[:, cache_half : 2 * cache_half].reshape(n_mlp * cache_half, HD)
    keys_new = arrived[:, 2 * cache_half : 2 * cache_half + new_half].reshape(n_mlp * new_half, HD)
    values_new = arrived[:, 2 * cache_half + new_half :].reshape(n_mlp * new_half, HD)
    pair = [(d, d ^ 1) for d in range(n_mlp)]
    partner_q = lax.ppermute(queries, "mlp", pair)
    grouped = jnp.concatenate([queries, partner_q], axis=1).reshape(query_rows, group_size, HD)
    score_scale = HD ** (-0.5)
    length = cache_len[0]
    cache_count = n_mlp * cache_half
    keys_all = jnp.concatenate([keys_old, keys_new], axis=0)
    values_all = jnp.concatenate([values_old, values_new], axis=0)
    cached_idx = lax.iota(jnp.int32, cache_count)
    cached_pos = (
        cached_idx // cache_half * cache_dev + my_half * cache_half + cached_idx % cache_half
    )
    new_idx = lax.iota(jnp.int32, n_mlp * new_half)
    new_pos = new_idx // new_half * rows_dev + my_half * new_half + new_idx % new_half
    token_ids = lax.iota(jnp.int32, query_rows)
    allowed = jnp.concatenate(
        [
            jnp.broadcast_to((cached_pos < length)[None, :], (query_rows, cache_count)),
            new_pos[None, :] <= token_ids[:, None],
        ],
        axis=1,
    )
    scores = (
        jnp.einsum("tqd,kd->qtk", grouped, keys_all, preferred_element_type=jnp.float32)
        * score_scale
    )
    scores = jnp.where(allowed[None], scores, -jnp.inf)
    row_max = jnp.max(scores, axis=-1)
    weights = jnp.exp(scores - row_max[..., None])
    row_sum = jnp.sum(weights, axis=-1)
    weighted = jnp.einsum(
        "qtk,kd->qtd", weights.astype(jnp.bfloat16), values_all, preferred_element_type=jnp.float32
    )
    sent = lax.ppermute(
        (weighted[heads_dev:], row_max[heads_dev:], row_sum[heads_dev:]), "mlp", pair
    )
    other_weighted, other_max, other_sum = sent
    mine_max = row_max[:heads_dev]
    top = jnp.maximum(mine_max, other_max)
    scale_a = jnp.exp(mine_max - top)
    scale_b = jnp.exp(other_max - top)
    total = row_sum[:heads_dev] * scale_a + other_sum * scale_b
    mixed = weighted[:heads_dev] * scale_a[..., None] + other_weighted * scale_b[..., None]
    attended = (mixed / total[..., None]).astype(jnp.bfloat16)
    attended = attended.transpose(1, 0, 2).reshape(query_rows, heads_dev * HD)
    partial_value = jnp.dot(attended, out_weight, preferred_element_type=jnp.float32)
    row_start = my_index * rows_dev
    head_sum = lax.psum(partial_value.astype(jnp.bfloat16), "mlp").astype(jnp.float32)
    stream = (residual.astype(jnp.float32) + head_sum).astype(jnp.bfloat16)
    stream_full = stream.astype(jnp.float32)
    factor = lax.rsqrt(jnp.mean(stream_full * stream_full, axis=-1, keepdims=True) + norm_eps)
    normed = (stream_full * factor * norm_gain.astype(jnp.float32)).astype(jnp.bfloat16)
    stream_rows = lax.dynamic_slice_in_dim(stream, row_start, rows_dev, 0)
    units = gate_weight.shape[1]
    width = -(-units // 128) * 128

    def padded(block):
        return jnp.pad(block, ((0, 0), (0, width - units)))

    weights_full = lax.all_gather(
        jnp.concatenate([padded(gate_weight), padded(up_weight), padded(down_weight)], axis=1),
        "req",
        axis=0,
        tiled=True,
    )
    both = jnp.dot(normed, weights_full[:, : 2 * width], preferred_element_type=jnp.float32)
    gate_sum = both[:, :width]
    up_sum = both[:, width:]
    hidden = (jax.nn.silu(gate_sum) * up_sum).astype(jnp.bfloat16)
    mlp_part = lax.dot_general(
        hidden,
        weights_full[:, 2 * width :],
        (((1,), (1,)), ((), ())),
        preferred_element_type=jnp.float32,
    )
    mlp_rows = lax.psum_scatter(
        mlp_part.astype(jnp.bfloat16), "mlp", scatter_dimension=0, tiled=True
    ).astype(jnp.float32)
    return (stream_rows.astype(jnp.float32) + mlp_rows).astype(jnp.bfloat16)


def solution(mesh):
    in_specs = (
        P("req", "mlp"),
        P(("req", "mlp"), None),
        P(("req", "mlp"), None),
        P("req", "mlp", None),
        P("req", "mlp", None),
        P("req"),
        P("req", None),
        P("mlp", None),
        P(),
        P("req", "mlp"),
        P("req", "mlp"),
        P("req", "mlp"),
    )
    out_specs = P(("req", "mlp"), None)
    return jax.shard_map(shards, mesh=mesh, in_specs=in_specs, out_specs=out_specs, check_vma=False)
```

profile of v0, /device:TPU:8, one launch (start us, length us, event | category | flops | bytes accessed | tf_op | source)
XLA Modules:
  0.0 349.7 jit_solution(10881288263603468844)
XLA Ops:
  7.4 1.3 copy.25
  8.7 0.1 copy.17
  8.8 0.1 copy.26
  9.0 0.1 copy.18
  9.2 1.1 pad_maximum_fusion
  10.3 15.2 %all-to-all-start = ((bf16[280,16,128]{2,0,1:T(8,128)(2,1)}), bf16[280,16,128]{2,0,1:T(8,128)(2,1)S(1)}, u32[]{:S(2)}, u32[]{:S(2)}) async-start(bf16[280,16,128]{2,0,1:T(8,128)(2,1)} %pad_maximum_fusion), calls=%async_computation | async-start | bytes 2293760 | tf_op jit(solution)/shard_map/all_to_all | solution.py:52
  25.6 0.2 copy.22
  25.7 3.8 %collective-permute-start = (bf16[384,256]{0,1:T(8,128)(2,1)S(1)}, bf16[384,256]{0,1:T(8,128)(2,1)}, u32[]{:S(2)}, u32[]{:S(2)}) collective-permute-start(bf16[384,256]{0,1:T(8,128)(2,1)S(1)} %copy.22), channel_id=1, source_target_pairs={{0,1},{1,0},{2,3},{3,2},{4,5},{5,4},{6,7},{7,6},{8,9},{9,8},{10,11... | collective-permute-start | bytes 589832 | tf_op jit(solution)/shard_map/ppermute | solution.py:60
  30.3 0.1 iota_compare_fusion.4
  30.4 2.1 pad_add_fusion
  32.5 48.9 %collective-permute-done = bf16[384,256]{0,1:T(8,128)(2,1)} collective-permute-done((bf16[384,256]{0,1:T(8,128)(2,1)S(1)}, bf16[384,256]{0,1:T(8,128)(2,1)}, u32[]{:S(2)}, u32[]{:S(2)}) %collective-permute-start) | collective-permute-done | bytes 196640 | tf_op jit(solution)/shard_map/ppermute | solution.py:60
  81.4 1.7 pad_maximum_fusion.1
  83.1 1.1 fusion.58
  84.3 4.0 %fusion.2 = (f32[4,384]{1,0:T(4,128)S(1)}, f32[2240,384,4]{1,0,2:T(8,128)S(1)}) fusion(pred[384,2240]{0,1:T(8,128)(4,1)S(1)} %pad_add_fusion, bf16[384,4,128]{0,2,1:T(8,128)(2,1)} %bitcast.74, bf16[192,128]{1,0:T(8,128)(2,1)S(1)} %reshape.106, bf16[2048,128]{1,0:T(8,128)(2,1)} %bitcast.73), kind=kOutput, calls=%fused_computation.4 | convolution fusion | flops 892271104 | bytes 15595520 | tf_op jit(solution)/shard_map/tqd,kd->qtk/dot_general | solution.py:82
  88.4 3.3 fusion.3
  91.7 1.6 copy-done.1
  93.4 2.2 collective-permute-start.2
  95.6 7.8 %fusion = f32[4,384]{1,0:T(4,128)S(1)} fusion(f32[2240,384,4]{1,0,2:T(8,128)} %copy-done.1, f32[4,384]{1,0:T(4,128)S(1)} %get-tuple-element.14, pred[384,2240]{0,1:T(8,128)(4,1)S(1)} %pad_add_fusion), kind=kLoop, calls=%fused_computation.2 | loop fusion | flops 13761024 | bytes 14635008 | tf_op jit(solution)/shard_map/reduce_sum | solution.py:88
  103.4 3.6 %collective-permute-start.3 = (f32[2,384]{1,0:T(2,128)S(1)}, f32[2,384]{1,0:T(2,128)S(1)}, u32[]{:S(2)}, u32[]{:S(2)}) collective-permute-start(f32[2,384]{1,0:T(2,128)S(1)} %slice.65), channel_id=1, source_target_pairs={{0,1},{1,0},{2,3},{3,2},{4,5},{5,4},{6,7},{7,6},{8,9},{9,8},{10,11... | collective-permute-start | bytes 9224 | tf_op jit(solution)/shard_map/ppermute | solution.py:92
  107.1 2.2 collective-permute-start.1
  109.3 3.2 collective-permute-done.1
  112.6 0.1 fusion.29
  112.7 2.1 convolution_convert_fusion.1
  114.8 0.0 all-gather.2.cloned.1.call-start
  114.9 0.8 fusion.31
  115.7 0.2 reduce-scatter.2.cloned.1.call-start
  115.9 142.1 %all-reduce.5.cloned.1.call-done = bf16[384,2560]{1,0:T(8,128)(2,1)} async-done(((bf16[384,2560]{1,0:T(8,128)(2,1)}), bf16[384,2560]{1,0:T(8,128)(2,1)}) %all-reduce.5.cloned.1.call-update) | async-done | bytes 1966096 | tf_op jit(solution)/shard_map/psum | solution.py:106
  258.0 3.0 fusion.8
  261.0 5.6 %fusion.6 = f32[384,1280]{1,0:T(8,128)S(1)} fusion(bf16[2560,1920]{1,0:T(8,128)(2,1)} %all-gather.2.cloned.1.call-done, bf16[384,2560]{1,0:T(8,128)(2,1)S(1)} %get-tuple-element.6, f32[2560]{0:T(1024)S(1)} %convert_element_type.54, f32[384]{0:T(512)S(1)} %add_rsqrt_fusion), kind=kOutput, calls=%fused_computation.7 | convolution fusion | flops 2520514560 | bytes 10497536 | tf_op jit(solution)/shard_map/dot_general | solution.py:124
  266.6 5.0 %convolution_convert_fusion = bf16[384,2560]{1,0:T(8,128)(2,1)} fusion(bf16[2560,1920]{1,0:T(8,128)(2,1)} %all-gather.2.cloned.1.call-done, f32[384,1280]{1,0:T(8,128)S(1)} %fusion.6), kind=kOutput, calls=%fused_computation.11 | convolution fusion | flops 1260748800 | bytes 7208960 | tf_op jit(solution)/shard_map/dot_general | solution.py:128
  271.6 69.1 %reduce-scatter.2.cloned.1.call-done = bf16[24,2560]{1,0:T(8,128)(2,1)} async-done(((bf16[384,2560]{1,0:T(8,128)(2,1)}), bf16[24,2560]{1,0:T(8,128)(2,1)}) %reduce-scatter.2.cloned.1.call-update) | async-done | bytes 122896 | tf_op jit(solution)/shard_map/reduce_scatter | solution.py:134
  340.7 1.6 add_convert_fusion.1
  (47 shorter events, 0.4 us)
Async XLA Ops:
  7.4 105.3 %copy-start = (bf16[256,2560]{1,0:T(8,128)(2,1)S(1)}, bf16[256,2560]{1,0:T(8,128)(2,1)}, u32[]{:S(2)}) copy-start(bf16[256,2560]{1,0:T(8,128)(2,1)} %param.19) | copy-start | bytes 3932164
  7.4 1.4 copy-start.2
  7.4 1.7 copy-start.8
  7.4 1.7 copy-start.9
  8.9 16.6 %copy-start.4 = (bf16[384,256]{1,0:T(8,128)(2,1)S(1)}, bf16[384,256]{1,0:T(8,128)(2,1)}, u32[]{:S(2)}) copy-start(bf16[384,256]{1,0:T(8,128)(2,1)} %param.12) | copy-start | bytes 589828
  10.3 72.8 %all-to-all-start = ((bf16[280,16,128]{2,0,1:T(8,128)(2,1)}), bf16[280,16,128]{2,0,1:T(8,128)(2,1)S(1)}, u32[]{:S(2)}, u32[]{:S(2)}) async-start(bf16[280,16,128]{2,0,1:T(8,128)(2,1)} %pad_maximum_fusion), calls=%async_computation | async-start | bytes 2293760 | tf_op jit(solution)/shard_map/all_to_all | solution.py:52
  25.5 232.5 %all-reduce.5.cloned.1.call-start = ((), (), s32[]{:S(2)}) async-start(), calls=%async_computation.2 | async-start | bytes 3932160 | tf_op jit(solution)/shard_map/psum | solution.py:106
  25.7 55.7 %collective-permute-start = (bf16[384,256]{0,1:T(8,128)(2,1)S(1)}, bf16[384,256]{0,1:T(8,128)(2,1)}, u32[]{:S(2)}, u32[]{:S(2)}) collective-permute-start(bf16[384,256]{0,1:T(8,128)(2,1)S(1)} %copy.22), channel_id=1, source_target_pairs={{0,1},{1,0},{2,3},{3,2},{4,5},{5,4},{6,7},{7,6},{8,9},{9,8},{10,11... | collective-permute-start | bytes 589832 | tf_op jit(solution)/shard_map/ppermute | solution.py:60
  84.3 4.1 %copy-start.3 = (bf16[16,128,128]{2,1,0:T(8,128)(2,1)S(1)}, bf16[16,128,128]{2,1,0:T(8,128)(2,1)}, u32[]{:S(2)}) copy-start(bf16[16,128,128]{2,1,0:T(8,128)(2,1)} %get-tuple-element.10) | copy-start | bytes 1572868
  88.4 5.0 %copy-start.1 = (f32[2240,384,4]{1,0,2:T(8,128)}, f32[2240,384,4]{1,0,2:T(8,128)S(1)}, u32[]{:S(2)}) copy-start(f32[2240,384,4]{1,0,2:T(8,128)S(1)} %get-tuple-element.15) | copy-start | bytes 41287684
  93.4 19.2 %collective-permute-start.2 = (f32[2,384,128]{1,2,0:T(8,128)S(1)}, f32[2,384,128]{1,2,0:T(8,128)S(1)}, u32[]{:S(2)}, u32[]{:S(2)}) collective-permute-start(f32[2,384,128]{1,2,0:T(8,128)S(1)} %slice.63), channel_id=1, source_target_pairs={{0,1},{1,0},{2,3},{3,2},{4,5},{5,4},{6,7},{7,6},{8,9},{9,8},{10,11... | collective-permute-start | bytes 1179656 | tf_op jit(solution)/shard_map/ppermute | solution.py:92
  103.4 5.9 %collective-permute-start.3 = (f32[2,384]{1,0:T(2,128)S(1)}, f32[2,384]{1,0:T(2,128)S(1)}, u32[]{:S(2)}, u32[]{:S(2)}) collective-permute-start(f32[2,384]{1,0:T(2,128)S(1)} %slice.65), channel_id=1, source_target_pairs={{0,1},{1,0},{2,3},{3,2},{4,5},{5,4},{6,7},{7,6},{8,9},{9,8},{10,11... | collective-permute-start | bytes 9224 | tf_op jit(solution)/shard_map/ppermute | solution.py:92
  107.1 5.5 %collective-permute-start.1 = (f32[2,384]{1,0:T(2,128)S(1)}, f32[2,384]{1,0:T(2,128)S(1)}, u32[]{:S(2)}, u32[]{:S(2)}) collective-permute-start(f32[2,384]{1,0:T(2,128)S(1)} %slice.62), channel_id=1, source_target_pairs={{0,1},{1,0},{2,3},{3,2},{4,5},{5,4},{6,7},{7,6},{8,9},{9,8},{10,11... | collective-permute-start | bytes 9224 | tf_op jit(solution)/shard_map/ppermute | solution.py:92
  112.6 2.3 copy-start.5
  112.6 2.3 copy-start.6
  112.6 2.3 copy-start.7
  112.7 3.2 copy-start.10
  114.8 146.2 %all-gather.2.cloned.1.call-start = ((), (), s32[]{:S(2)}) async-start(), calls=%async_computation.3 | async-start | bytes 10137600 | tf_op jit(solution)/shard_map/all_gather | solution.py:118
  115.7 225.0 %reduce-scatter.2.cloned.1.call-start = ((), (), s32[]{:S(2)}) async-start(), calls=%async_computation.4 | async-start | bytes 2088960 | tf_op jit(solution)/shard_map/reduce_scatter | solution.py:134
Sparse Core Ops, SparseCore 0:
  114.9 143.0 all-reduce.4
  271.8 68.8 reduce-scatter.1
Sparse Core Ops, SparseCore 1:
  119.0 70.9 all-gather.1
where the time goes:
time: 350 us
  waiting for transfers between devices  263 us (75%)
  starting transfers between devices  27.4 us (8%)
  matrix products  20 us (6%)
  other arithmetic  18.4 us (5%)
  between operations  15.9 us (5%)
  local copies, waits for them, and re-layouts  4.71 us (1%)
    psum x1, waiting for transfers between devices, shards(): lax.psum(partial_value.astype(jnp.bfloat16), 'mlp').astype(jnp.float32)  142 us
    reduce_scatter x1, waiting for transfers between devices, shards(): lax.psum_scatter(mlp_part.astype(jnp.bfloat16), 'mlp', scatter_dimension=...  69.1 us
    ppermute x1, waiting for transfers between devices, shards(): partner_q = lax.ppermute(queries, 'mlp', pair)  48.9 us
    all_to_all x1, starting transfers between devices, shards(): lax.all_to_all(send, 'mlp', split_axis=1, concat_axis=0, tiled=True)  15.2 us
    ppermute x3, starting transfers between devices, shards(): lax.ppermute((weighted[heads_dev:], row_max[heads_dev:], row_sum[heads_de...  8.08 us
    reduce_sum x1, other arithmetic, shards(): row_sum = jnp.sum(weights, axis=-1)  7.81 us
  transfers between devices with their start and end apart: 8, of which 4 were waited for; matrix products, arithmetic and copies ran while one was open for 5% of the time, Pallas kernels for 0%

commit v1 on v0

--- a/solution.py
+++ b/solution.py
@@ -103,7 +103,9 @@
     attended = attended.transpose(1, 0, 2).reshape(query_rows, heads_dev * HD)
     partial_value = jnp.dot(attended, out_weight, preferred_element_type=jnp.float32)
     row_start = my_index * rows_dev
-    head_sum = lax.psum(partial_value.astype(jnp.bfloat16), "mlp").astype(jnp.float32)
+    head_sum = jnp.sum(lax.all_gather(partial_value.astype(jnp.bfloat16), "mlp"), axis=0).astype(
+        jnp.float32
+    )
     stream = (residual.astype(jnp.float32) + head_sum).astype(jnp.bfloat16)
     stream_full = stream.astype(jnp.float32)
     factor = lax.rsqrt(jnp.mean(stream_full * stream_full, axis=-1, keepdims=True) + norm_eps)

time: 350 us -> 617 us (1.76)
  the two profiles are of different devices: /device:TPU:8 before, /device:TPU:2 now
where the time goes in v1:
time: 617 us; the launch traced here: 616 us
  waiting for transfers between devices  519 us (84%)
  other arithmetic  30.4 us (5%)
  starting transfers between devices  27.4 us (4%)
  matrix products  20.6 us (3%)
  between operations  14.2 us (2%)
    all_gather x1, waiting for transfers between devices, shards(): lax.all_gather(partial_value.astype(jnp.bfloat16), 'mlp')  336 us
    reduce_scatter x1, waiting for transfers between devices, shards(): lax.psum_scatter(mlp_part.astype(jnp.bfloat16), 'mlp', scatter_dimension=...  72.7 us
    all_gather x1, waiting for transfers between devices, shards(): lax.all_gather(jnp.concatenate([padded(gate_weight), padded(up_weight), p...  57.8 us
    ppermute x1, waiting for transfers between devices, shards(): partner_q = lax.ppermute(queries, 'mlp', pair)  48.9 us
    all_to_all x1, starting transfers between devices, shards(): lax.all_to_all(send, 'mlp', split_axis=1, concat_axis=0, tiled=True)  15.2 us
  transfers between devices with their start and end apart: 8, of which 5 were waited for; matrix products, arithmetic and copies ran while one was open for 4% of the time, Pallas kernels for 0%

profile of v1, /device:TPU:2, one launch (start us, length us, event | category | flops | bytes accessed | tf_op | source)
XLA Modules:
  0.0 616.4 jit_solution(11347363976886414935)
XLA Ops:
  6.5 1.3 copy.25
  7.9 0.1 copy.17
  8.0 0.1 copy.26
  8.1 0.1 copy.18
  8.3 1.1 pad_maximum_fusion
  9.5 15.2 %all-to-all-start = ((bf16[280,16,128]{2,0,1:T(8,128)(2,1)}), bf16[280,16,128]{2,0,1:T(8,128)(2,1)S(1)}, u32[]{:S(2)}, u32[]{:S(2)}) async-start(bf16[280,16,128]{2,0,1:T(8,128)(2,1)} %pad_maximum_fusion), calls=%async_computation | async-start | bytes 2293760 | tf_op jit(solution)/shard_map/all_to_all | solution.py:52
  24.7 0.2 copy.22
  24.9 3.8 collective-permute-start
  29.4 0.1 iota_compare_fusion.4
  29.6 2.1 pad_add_fusion
  31.7 48.9 %collective-permute-done = bf16[384,256]{0,1:T(8,128)(2,1)} collective-permute-done((bf16[384,256]{0,1:T(8,128)(2,1)S(1)}, bf16[384,256]{0,1:T(8,128)(2,1)}, u32[]{:S(2)}, u32[]{:S(2)}) %collective-permute-start) | collective-permute-done | bytes 196640 | tf_op jit(solution)/shard_map/ppermute | solution.py:60
  80.6 1.7 pad_maximum_fusion.1
  82.3 1.1 fusion.58
  83.5 4.0 fusion.2
  87.5 3.3 fusion.3
  90.9 1.6 copy-done.2
  92.5 2.2 collective-permute-start.2
  94.8 7.8 %fusion = f32[4,384]{1,0:T(4,128)S(1)} fusion(f32[2240,384,4]{1,0,2:T(8,128)} %copy-done.2, f32[4,384]{1,0:T(4,128)S(1)} %get-tuple-element.14, pred[384,2240]{0,1:T(8,128)(4,1)S(1)} %pad_add_fusion), kind=kLoop, calls=%fused_computation.2 | loop fusion | flops 13761024 | bytes 14635008 | tf_op jit(solution)/shard_map/reduce_sum | solution.py:88
  102.6 3.6 collective-permute-start.3
  106.2 2.2 collective-permute-start.1
  108.5 3.2 collective-permute-done.1
  111.9 2.0 convolution_convert_fusion.1
  114.0 0.7 fusion.31
  114.7 0.2 reduce-scatter.2.cloned.1.call-start
  115.0 336.5 %all-gather.6.cloned.1.call-done = bf16[6144,2560]{1,0:T(8,128)(2,1)} async-done(((bf16[384,2560]{1,0:T(8,128)(2,1)}), bf16[6144,2560]{1,0:T(8,128)(2,1)}) %all-gather.6.cloned.1.call-update) | async-done | bytes 31457296 | tf_op jit(solution)/shard_map/all_gather | solution.py:106
  451.5 11.3 %reduce_sum.31 = bf16[384,2560]{1,0:T(8,128)(2,1)S(1)} reduce(bf16[16,384,2560]{2,1,0:T(8,128)(2,1)} %bitcast.64, bf16[]{:T(256)} %constant.83.clone.1), dimensions={0}, to_apply=%region_2.3 | reduce | flops 14745600 | bytes 33423362 | tf_op jit(solution)/shard_map/reduce_sum | solution.py:106
  462.8 3.7 fusion.8
  466.4 57.8 %all-gather.4.cloned.1.call-done = bf16[2560,1920]{1,0:T(8,128)(2,1)} async-done(((bf16[80,1920]{1,0:T(8,128)(2,1)}), bf16[2560,1920]{1,0:T(8,128)(2,1)}) %all-gather.4.cloned.1.call-update) | async-done | bytes 9830416 | tf_op jit(solution)/shard_map/all_gather | solution.py:120
  524.3 6.2 %fusion.6 = f32[384,1280]{1,0:T(8,128)S(1)} fusion(bf16[2560,1920]{1,0:T(8,128)(2,1)} %all-gather.4.cloned.1.call-done, bf16[384,2560]{1,0:T(8,128)(2,1)} %get-tuple-element.6, f32[2560]{0:T(1024)S(1)} %convert_element_type.56, f32[384]{0:T(512)S(1)} %add_rsqrt_fusion), kind=kOutput, calls=%fused_computation.7 | convolution fusion | flops 2520514560 | bytes 10497536 | tf_op jit(solution)/shard_map/dot_general | solution.py:126
  530.5 5.0 convolution_convert_fusion
  535.5 72.7 %reduce-scatter.2.cloned.1.call-done = bf16[24,2560]{1,0:T(8,128)(2,1)} async-done(((bf16[384,2560]{1,0:T(8,128)(2,1)}), bf16[24,2560]{1,0:T(8,128)(2,1)}) %reduce-scatter.2.cloned.1.call-update) | async-done | bytes 122896 | tf_op jit(solution)/shard_map/reduce_scatter | solution.py:136
  608.2 1.6 add_convert_fusion.1
  (50 shorter events, 0.5 us)
Async XLA Ops:
  6.5 105.3 %copy-start = (bf16[256,2560]{1,0:T(8,128)(2,1)S(1)}, bf16[256,2560]{1,0:T(8,128)(2,1)}, u32[]{:S(2)}) copy-start(bf16[256,2560]{1,0:T(8,128)(2,1)} %param.19) | copy-start | bytes 3932164
  6.5 1.4 copy-start.3
  6.5 1.7 copy-start.9
  6.5 1.7 copy-start.10
  8.1 16.6 %copy-start.5 = (bf16[384,256]{1,0:T(8,128)(2,1)S(1)}, bf16[384,256]{1,0:T(8,128)(2,1)}, u32[]{:S(2)}) copy-start(bf16[384,256]{1,0:T(8,128)(2,1)} %param.12) | copy-start | bytes 589828
  9.5 72.8 %all-to-all-start = ((bf16[280,16,128]{2,0,1:T(8,128)(2,1)}), bf16[280,16,128]{2,0,1:T(8,128)(2,1)S(1)}, u32[]{:S(2)}, u32[]{:S(2)}) async-start(bf16[280,16,128]{2,0,1:T(8,128)(2,1)} %pad_maximum_fusion), calls=%async_computation | async-start | bytes 2293760 | tf_op jit(solution)/shard_map/all_to_all | solution.py:52
  24.7 426.8 %all-gather.6.cloned.1.call-start = ((), (), s32[]{:S(2)}) async-start(), calls=%async_computation.4 | async-start | bytes 33423360 | tf_op jit(solution)/shard_map/all_gather | solution.py:106
  24.9 55.7 %collective-permute-start = (bf16[384,256]{0,1:T(8,128)(2,1)S(1)}, bf16[384,256]{0,1:T(8,128)(2,1)}, u32[]{:S(2)}, u32[]{:S(2)}) collective-permute-start(bf16[384,256]{0,1:T(8,128)(2,1)S(1)} %copy.22), channel_id=1, source_target_pairs={{0,1},{1,0},{2,3},{3,2},{4,5},{5,4},{6,7},{7,6},{8,9},{9,8},{10,11... | collective-permute-start | bytes 589832 | tf_op jit(solution)/shard_map/ppermute | solution.py:60
  83.5 4.1 copy-start.4
  87.5 5.0 copy-start.2
  92.5 19.2 %collective-permute-start.2 = (f32[2,384,128]{1,2,0:T(8,128)S(1)}, f32[2,384,128]{1,2,0:T(8,128)S(1)}, u32[]{:S(2)}, u32[]{:S(2)}) collective-permute-start(f32[2,384,128]{1,2,0:T(8,128)S(1)} %slice.63), channel_id=1, source_target_pairs={{0,1},{1,0},{2,3},{3,2},{4,5},{5,4},{6,7},{7,6},{8,9},{9,8},{10,11... | collective-permute-start | bytes 1179656 | tf_op jit(solution)/shard_map/ppermute | solution.py:92
  102.6 5.9 collective-permute-start.3
  106.2 5.5 collective-permute-start.1
  111.7 2.2 copy-start.6
  111.7 2.2 copy-start.7
  111.8 2.2 copy-start.8
  111.9 3.1 copy-start.11
  113.9 410.4 %all-gather.4.cloned.1.call-start = ((), (), s32[]{:S(2)}) async-start(), calls=%async_computation.2 | async-start | bytes 10137600 | tf_op jit(solution)/shard_map/all_gather | solution.py:120
  114.7 493.5 %reduce-scatter.2.cloned.1.call-start = ((), (), s32[]{:S(2)}) async-start(), calls=%async_computation.3 | async-start | bytes 2088960 | tf_op jit(solution)/shard_map/reduce_scatter | solution.py:136
  530.5 79.4 %copy-start.1 = (bf16[256,2560]{1,0:T(8,128)(2,1)S(1)}, bf16[256,2560]{1,0:T(8,128)(2,1)}, u32[]{:S(2)}) copy-start(bf16[256,2560]{1,0:T(8,128)(2,1)} %param.19) | copy-start | bytes 3932164
Sparse Core Ops, SparseCore 0:
  114.0 337.4 all-gather.5
  454.7 69.5 all-gather.3
  535.7 72.4 reduce-scatter.1
